TPU v7x, 512 devices: a whole 4x8x8 slice. The times are simulated.
512 devices in a mesh: section: 8 (over x, core), tile: 64 (over z, y).
Axes of the slice: x: 4, y: 8, z: 8, core: 2. Of those that a mesh axis runs over, the one named last changes fastest.
Arguments:
- latents: bfloat16 [8, 2, 512, 384], P(None, None, 'tile'), may hold values from -6 to 6
- col_counts: int32 [64], replicated, may hold values from 1 to 8, 480 in all
- conv_weight: bfloat16 [8, 3, 3, 1152, 384], P('section'), may hold values from -0.0625 to 0.0625
- norm_gain: bfloat16 [8, 384], P('section'), may hold values from 0.099609375 to 1.8984375
Outputs:
- decoded: bfloat16 [8, 2, 512, 384], P('section', None, 'tile')
Inputs may be any that keep to these rules, and one draw needn't show every extreme that they name: Strip t holds col_counts[t] image columns; the counts sum to 480 and some strip holds 8.
All inputs are finite; a program needn't handle non-finite values.
Results may differ from a plain program's by a relative error of at most 0.013.
Values may be sent and summed in bfloat16 or wider, within the bound.
No kernel may reach another device: no remote copies, remote signals or barrier semaphores. Data moves between devices by JAX's collectives and lax.ppermute only.
A program may use at most 64 MiB of HBM per device.

v0:
```python
import jax
import jax.numpy as jnp
from jax import lax
from jax.sharding import PartitionSpec as P

SPAN_T = 4


def padded(block, sides, width):
    for axis, dim in sides:
        count = lax.axis_size(axis)
        forward = [(i, i + 1) for i in range(count - 1)]
        backward = [(target, source) for source, target in forward]
        low = lax.ppermute(
            lax.slice_in_dim(block, block.shape[dim] - width, None, axis=dim), axis, forward
        )
        high = lax.ppermute(lax.slice_in_dim(block, 0, width, axis=dim), axis, backward)
        block = jnp.concatenate([low, block, high], axis=dim)
    return block


def passed_along(block, axis, distance):
    devices = range(lax.axis_size(axis))
    route = [(i - distance, i) for i in devices if i - distance in devices]
    return lax.ppermute(block, axis, route)


def from_root(shard, axis, root):
    mine = lax.axis_index(axis) == root
    return lax.psum(jnp.where(mine, shard, jnp.zeros_like(shard)), axis)


def convolve(sequence, kernel, frame_depth, row_count, col_count):
    joined = jnp.concatenate(
        [
            sequence[:, :, 0:col_count],
            sequence[:, :, 1 : col_count + 1],
            sequence[:, :, 2 : col_count + 2],
        ],
        axis=-1,
    )
    summed = jnp.zeros((frame_depth, row_count, col_count, kernel.shape[-1]), jnp.float32)
    for frame_tap in range(3):
        for row_tap in range(3):
            summed = summed + jnp.dot(
                joined[frame_tap : frame_tap + frame_depth, row_tap : row_tap + row_count],
                kernel[frame_tap, row_tap],
                preferred_element_type=jnp.float32,
            )
    return summed


def local(latents, col_counts, conv_weight, norm_gain):
    segments = lax.axis_size("section")
    segment_index = lax.axis_index("section")
    tile_index = lax.axis_index("tile")
    frames_all, row_count, col_count, channels = latents.shape
    live_cols = col_counts[tile_index]
    kernel = conv_weight[0]
    norm_scale = norm_gain[0].astype(jnp.float32)
    frame_depth = SPAN_T
    pieces = frames_all // frame_depth
    total_steps = pieces + segments - 1
    col_live = jnp.arange(col_count)[None, None, :, None] < live_cols
    col_index = jnp.arange(col_count + 2)[None, None, :, None]
    even_segment = segment_index % 2 == 0
    last_segment = segment_index == segments - 1
    zero_value = jnp.zeros((), jnp.bfloat16)

    def advance(step_index, carried):
        inbound, memory, result = carried
        micro_index = step_index - segment_index
        active = (micro_index >= 0) & (micro_index < pieces)
        frame_start = jnp.clip(micro_index, 0, pieces - 1) * frame_depth
        entering = lax.dynamic_slice_in_dim(latents, frame_start, frame_depth, 0)
        residual = jnp.where(
            col_live, jnp.where(segment_index == 0, entering, inbound[0]), zero_value
        )
        branch = inbound[1]
        source = jnp.where(even_segment, residual, branch).astype(jnp.float32)
        normed = (
            source
            * lax.rsqrt(jnp.mean(source * source, axis=-1, keepdims=True) + 1e-06)
            * norm_scale
        )
        activated = jnp.where(col_live, jax.nn.silu(normed), 0.0).astype(jnp.bfloat16)
        first_col = activated[:, :, 0:1]
        last_col = lax.dynamic_slice_in_dim(activated, live_cols - 1, 1, 2)
        haloed = padded(jnp.concatenate([first_col, last_col], axis=2), (("tile", 2),), 1)
        widened = jnp.concatenate([haloed[:, :, 0:1], activated, jnp.zeros_like(first_col)], axis=2)
        widened = jnp.where(col_index == live_cols + 1, haloed[:, :, 3:4], widened)
        extended = jnp.pad(widened, ((0, 0), (1, 1), (0, 0), (0, 0)))
        sequence = jnp.concatenate([memory, extended], axis=0)
        memory = jnp.where(active, sequence[-2:], memory)
        conv_out = jnp.where(
            col_live, convolve(sequence, kernel, frame_depth, row_count, col_count), 0.0
        )
        resid_next = jnp.where(
            even_segment, residual, (residual.astype(jnp.float32) + conv_out).astype(jnp.bfloat16)
        )
        branch_next = jnp.where(even_segment, conv_out.astype(jnp.bfloat16), branch)
        written = lax.dynamic_update_slice_in_dim(result, resid_next, frame_start, 0)
        result = jnp.where(active & last_segment, written, result)
        inbound = passed_along(jnp.stack([resid_next, branch_next]), "section", 1)
        return (inbound, memory, result)

    inbound = jnp.zeros((2, frame_depth, row_count, col_count, channels), jnp.bfloat16)
    memory = jnp.zeros((2, row_count + 2, col_count + 2, channels), jnp.bfloat16)
    result = jnp.zeros((frames_all, row_count, col_count, channels), jnp.bfloat16)
    inbound, memory, result = lax.fori_loop(0, total_steps, advance, (inbound, memory, result))
    gathered = from_root(result, "section", segments - 1)
    frame_share = frames_all // segments
    return lax.dynamic_slice_in_dim(gathered, segment_index * frame_share, frame_share, 0)


def solution(mesh):
    return jax.shard_map(
        local,
        mesh=mesh,
        in_specs=(
            P(None, None, "tile", None),
            P(),
            P("section", None, None, None, None),
            P("section", None),
        ),
        out_specs=P("section", None, "tile", None),
        check_vma=False,
    )
```

profile of v0, /device:TPU:8, one launch (start us, length us, event | category | flops | bytes accessed | tf_op | source)
XLA Modules:
  0.0 376.8 jit_solution(10968144452210081428)
XLA Ops:
  10.5 269.9 %while.20 = (s32[]{:T(128)}, bf16[2,4,2,8,384]{4,3,2,1,0:T(8,128)(2,1)S(1)}, bf16[2,4,10,384]{3,2,1,0:T(8,128)(2,1)S(1)}, bf16[8,2,8,384]{3,2,1,0:T(8,128)(2,1)S...) while((s32[]{:T(128)}, ...), condition=%wide.region_2.3_spmd.clone, body=%wide.region_0.2_spmd.clone.sunk | while | flops 512637024 | bytes 16789532 | solution.py:110
  12.3 3.5 collective-permute-start
  15.8 5.5 %collective-permute-start.1 = (bf16[4,2,1,384]{3,2,1,0:T(2,128)(2,1)S(1)}, bf16[4,2,1,384]{3,2,1,0:T(2,128)(2,1)S(1)}, u32[]{:S(2)}, u32[]{:S(2)}) collective-permute-start(bf16[4,2,1,384]{3,2,1,0:T(2,128)(2,1)S(1)} %get-tuple-element.519), channel_id=1, source_target_pairs={{1,0},{2,1},{3,2},{4,3},{5,4},{6,5},{7,6},{8,7},{9,8},{10,9},{11,1... | collective-permute-start | bytes 18440 | tf_op jit(solution)/shard_map/while/body/eval_jaxpr/ppermute | solution.py:17
  26.0 1.4 convolution_add_fusion.16
  27.4 1.4 convolution_add_fusion.17
  28.8 1.4 convolution_add_fusion.18
  34.6 1.5 select_dynamic-update-slice_fusion.2
  40.1 2.9 collective-permute-start
  43.0 2.9 collective-permute-start.1
  46.0 3.8 collective-permute-done.1
  61.7 1.5 select_dynamic-update-slice_fusion.2
  63.2 3.7 collective-permute-start.2
  69.6 3.6 collective-permute-start
  73.2 2.2 collective-permute-start.1
  75.5 3.3 collective-permute-done.1
  90.6 1.5 select_dynamic-update-slice_fusion.2
  92.1 5.0 %collective-permute-start.2 = (bf16[2,4,2,8,384]{4,3,2,1,0:T(8,128)(2,1)S(1)}, bf16[2,4,2,8,384]{4,3,2,1,0:T(8,128)(2,1)S(1)}, u32[]{:S(2)}, u32[]{:S(2)}) collective-permute-start(bf16[2,4,2,8,384]{4,3,2,1,0:T(8,128)(2,1)S(1)} %pad_maximum_fusion.3), channel_id=1, source_target_pairs={{0,64},{64,128},{128,192},{192,256},{256,320},{320,384},{384,448},... | collective-permute-start | bytes 294920 | tf_op jit(solution)/shard_map/while/body/eval_jaxpr/ppermute | solution.py:25
  99.9 3.1 collective-permute-start
  103.0 2.7 collective-permute-start.1
  105.8 2.8 collective-permute-done.1
  120.5 1.5 select_dynamic-update-slice_fusion.2
  121.9 5.0 %collective-permute-start.2 = (bf16[2,4,2,8,384]{4,3,2,1,0:T(8,128)(2,1)S(1)}, bf16[2,4,2,8,384]{4,3,2,1,0:T(8,128)(2,1)S(1)}, u32[]{:S(2)}, u32[]{:S(2)}) collective-permute-start(bf16[2,4,2,8,384]{4,3,2,1,0:T(8,128)(2,1)S(1)} %pad_maximum_fusion.3), channel_id=1, source_target_pairs={{0,64},{64,128},{128,192},{192,256},{256,320},{320,384},{384,448},... | collective-permute-start | bytes 294920 | tf_op jit(solution)/shard_map/while/body/eval_jaxpr/ppermute | solution.py:25
  129.7 3.1 collective-permute-start
  132.8 2.7 collective-permute-start.1
  135.6 2.8 collective-permute-done.1
  150.3 1.5 select_dynamic-update-slice_fusion.2
  151.8 5.0 %collective-permute-start.2 = (bf16[2,4,2,8,384]{4,3,2,1,0:T(8,128)(2,1)S(1)}, bf16[2,4,2,8,384]{4,3,2,1,0:T(8,128)(2,1)S(1)}, u32[]{:S(2)}, u32[]{:S(2)}) collective-permute-start(bf16[2,4,2,8,384]{4,3,2,1,0:T(8,128)(2,1)S(1)} %pad_maximum_fusion.3), channel_id=1, source_target_pairs={{0,64},{64,128},{128,192},{192,256},{256,320},{320,384},{384,448},... | collective-permute-start | bytes 294920 | tf_op jit(solution)/shard_map/while/body/eval_jaxpr/ppermute | solution.py:25
  159.5 3.2 collective-permute-start
  162.7 2.7 collective-permute-start.1
  165.4 2.9 collective-permute-done.1
  180.2 1.5 select_dynamic-update-slice_fusion.2
  181.7 5.3 %collective-permute-start.2 = (bf16[2,4,2,8,384]{4,3,2,1,0:T(8,128)(2,1)S(1)}, bf16[2,4,2,8,384]{4,3,2,1,0:T(8,128)(2,1)S(1)}, u32[]{:S(2)}, u32[]{:S(2)}) collective-permute-start(bf16[2,4,2,8,384]{4,3,2,1,0:T(8,128)(2,1)S(1)} %pad_maximum_fusion.3), channel_id=1, source_target_pairs={{0,64},{64,128},{128,192},{192,256},{256,320},{320,384},{384,448},... | collective-permute-start | bytes 294920 | tf_op jit(solution)/shard_map/while/body/eval_jaxpr/ppermute | solution.py:25
  189.7 3.6 collective-permute-start
  193.4 2.2 collective-permute-start.1
  195.7 3.4 collective-permute-done.1
  210.9 1.5 select_dynamic-update-slice_fusion.2
  212.4 5.3 %collective-permute-start.2 = (bf16[2,4,2,8,384]{4,3,2,1,0:T(8,128)(2,1)S(1)}, bf16[2,4,2,8,384]{4,3,2,1,0:T(8,128)(2,1)S(1)}, u32[]{:S(2)}, u32[]{:S(2)}) collective-permute-start(bf16[2,4,2,8,384]{4,3,2,1,0:T(8,128)(2,1)S(1)} %pad_maximum_fusion.3), channel_id=1, source_target_pairs={{0,64},{64,128},{128,192},{192,256},{256,320},{320,384},{384,448},... | collective-permute-start | bytes 294920 | tf_op jit(solution)/shard_map/while/body/eval_jaxpr/ppermute | solution.py:25
  220.4 3.6 collective-permute-start
  224.1 2.2 collective-permute-start.1
  226.4 3.7 collective-permute-done.1
  242.0 1.5 select_dynamic-update-slice_fusion.2
  243.5 5.3 %collective-permute-start.2 = (bf16[2,4,2,8,384]{4,3,2,1,0:T(8,128)(2,1)S(1)}, bf16[2,4,2,8,384]{4,3,2,1,0:T(8,128)(2,1)S(1)}, u32[]{:S(2)}, u32[]{:S(2)}) collective-permute-start(bf16[2,4,2,8,384]{4,3,2,1,0:T(8,128)(2,1)S(1)} %pad_maximum_fusion.3), channel_id=1, source_target_pairs={{0,64},{64,128},{128,192},{192,256},{256,320},{320,384},{384,448},... | collective-permute-start | bytes 294920 | tf_op jit(solution)/shard_map/while/body/eval_jaxpr/ppermute | solution.py:25
  251.5 3.6 collective-permute-start
  255.1 2.2 collective-permute-start.1
  257.4 3.4 collective-permute-done.1
  272.7 1.5 select_dynamic-update-slice_fusion.2
  274.2 5.3 %collective-permute-start.2 = (bf16[2,4,2,8,384]{4,3,2,1,0:T(8,128)(2,1)S(1)}, bf16[2,4,2,8,384]{4,3,2,1,0:T(8,128)(2,1)S(1)}, u32[]{:S(2)}, u32[]{:S(2)}) collective-permute-start(bf16[2,4,2,8,384]{4,3,2,1,0:T(8,128)(2,1)S(1)} %pad_maximum_fusion.3), channel_id=1, source_target_pairs={{0,64},{64,128},{128,192},{192,256},{256,320},{320,384},{384,448},... | collective-permute-start | bytes 294920 | tf_op jit(solution)/shard_map/while/body/eval_jaxpr/ppermute | solution.py:25
  281.1 87.6 %all-reduce.3.cloned.1.call-done = bf16[8,2,8,384]{3,2,1,0:T(8,128)(2,1)} async-done(((bf16[8,2,8,384]{3,2,1,0:T(8,128)(2,1)}), bf16[8,2,8,384]{3,2,1,0:T(8,128)(2,1)}) %all-reduce.3.cloned.1.call-update) | async-done | bytes 98320 | tf_op jit(solution)/shard_map/psum | solution.py:30
  (224 shorter events, 133.1 us)
Async XLA Ops:
  6.5 362.1 %all-reduce.3.cloned.1.call-start = ((), (), s32[]{:S(2)}) async-start(), calls=%async_computation | async-start | bytes 196608 | tf_op jit(solution)/shard_map/psum | solution.py:30
  12.3 10.4 %collective-permute-start = (bf16[4,2,1,384]{3,2,1,0:T(2,128)(2,1)S(1)}, bf16[4,2,1,384]{3,2,1,0:T(2,128)(2,1)S(1)}, u32[]{:S(2)}, u32[]{:S(2)}) collective-permute-start(bf16[4,2,1,384]{3,2,1,0:T(2,128)(2,1)S(1)} %get-tuple-element.518), channel_id=1, source_target_pairs={{0,1},{1,2},{2,3},{3,4},{4,5},{5,6},{6,7},{7,8},{8,9},{9,10},{10,1... | collective-permute-start | bytes 18440 | tf_op jit(solution)/shard_map/while/body/eval_jaxpr/ppermute | solution.py:14
  15.8 6.9 %collective-permute-start.1 = (bf16[4,2,1,384]{3,2,1,0:T(2,128)(2,1)S(1)}, bf16[4,2,1,384]{3,2,1,0:T(2,128)(2,1)S(1)}, u32[]{:S(2)}, u32[]{:S(2)}) collective-permute-start(bf16[4,2,1,384]{3,2,1,0:T(2,128)(2,1)S(1)} %get-tuple-element.519), channel_id=1, source_target_pairs={{1,0},{2,1},{3,2},{4,3},{5,4},{6,5},{7,6},{8,7},{9,8},{10,9},{11,1... | collective-permute-start | bytes 18440 | tf_op jit(solution)/shard_map/while/body/eval_jaxpr/ppermute | solution.py:17
  36.1 2.2 collective-permute-start.2
  40.1 9.7 %collective-permute-start = (bf16[4,2,1,384]{3,2,1,0:T(2,128)(2,1)S(1)}, bf16[4,2,1,384]{3,2,1,0:T(2,128)(2,1)S(1)}, u32[]{:S(2)}, u32[]{:S(2)}) collective-permute-start(bf16[4,2,1,384]{3,2,1,0:T(2,128)(2,1)S(1)} %get-tuple-element.518), channel_id=1, source_target_pairs={{0,1},{1,2},{2,3},{3,4},{4,5},{5,6},{6,7},{7,8},{8,9},{9,10},{10,1... | collective-permute-start | bytes 18440 | tf_op jit(solution)/shard_map/while/body/eval_jaxpr/ppermute | solution.py:14
  43.0 6.8 %collective-permute-start.1 = (bf16[4,2,1,384]{3,2,1,0:T(2,128)(2,1)S(1)}, bf16[4,2,1,384]{3,2,1,0:T(2,128)(2,1)S(1)}, u32[]{:S(2)}, u32[]{:S(2)}) collective-permute-start(bf16[4,2,1,384]{3,2,1,0:T(2,128)(2,1)S(1)} %get-tuple-element.519), channel_id=1, source_target_pairs={{1,0},{2,1},{3,2},{4,3},{5,4},{6,5},{7,6},{8,7},{9,8},{10,9},{11,1... | collective-permute-start | bytes 18440 | tf_op jit(solution)/shard_map/while/body/eval_jaxpr/ppermute | solution.py:17
  63.2 4.6 %collective-permute-start.2 = (bf16[2,4,2,8,384]{4,3,2,1,0:T(8,128)(2,1)S(1)}, bf16[2,4,2,8,384]{4,3,2,1,0:T(8,128)(2,1)S(1)}, u32[]{:S(2)}, u32[]{:S(2)}) collective-permute-start(bf16[2,4,2,8,384]{4,3,2,1,0:T(8,128)(2,1)S(1)} %pad_maximum_fusion.3), channel_id=1, source_target_pairs={{0,64},{64,128},{128,192},{192,256},{256,320},{320,384},{384,448},... | collective-permute-start | bytes 294920 | tf_op jit(solution)/shard_map/while/body/eval_jaxpr/ppermute | solution.py:25
  69.6 9.3 %collective-permute-start = (bf16[4,2,1,384]{3,2,1,0:T(2,128)(2,1)S(1)}, bf16[4,2,1,384]{3,2,1,0:T(2,128)(2,1)S(1)}, u32[]{:S(2)}, u32[]{:S(2)}) collective-permute-start(bf16[4,2,1,384]{3,2,1,0:T(2,128)(2,1)S(1)} %get-tuple-element.518), channel_id=1, source_target_pairs={{0,1},{1,2},{2,3},{3,4},{4,5},{5,6},{6,7},{7,8},{8,9},{9,10},{10,1... | collective-permute-start | bytes 18440 | tf_op jit(solution)/shard_map/while/body/eval_jaxpr/ppermute | solution.py:14
  73.2 5.6 %collective-permute-start.1 = (bf16[4,2,1,384]{3,2,1,0:T(2,128)(2,1)S(1)}, bf16[4,2,1,384]{3,2,1,0:T(2,128)(2,1)S(1)}, u32[]{:S(2)}, u32[]{:S(2)}) collective-permute-start(bf16[4,2,1,384]{3,2,1,0:T(2,128)(2,1)S(1)} %get-tuple-element.519), channel_id=1, source_target_pairs={{1,0},{2,1},{3,2},{4,3},{5,4},{6,5},{7,6},{8,7},{9,8},{10,9},{11,1... | collective-permute-start | bytes 18440 | tf_op jit(solution)/shard_map/while/body/eval_jaxpr/ppermute | solution.py:17
  92.1 5.9 %collective-permute-start.2 = (bf16[2,4,2,8,384]{4,3,2,1,0:T(8,128)(2,1)S(1)}, bf16[2,4,2,8,384]{4,3,2,1,0:T(8,128)(2,1)S(1)}, u32[]{:S(2)}, u32[]{:S(2)}) collective-permute-start(bf16[2,4,2,8,384]{4,3,2,1,0:T(8,128)(2,1)S(1)} %pad_maximum_fusion.3), channel_id=1, source_target_pairs={{0,64},{64,128},{128,192},{192,256},{256,320},{320,384},{384,448},... | collective-permute-start | bytes 294920 | tf_op jit(solution)/shard_map/while/body/eval_jaxpr/ppermute | solution.py:25
  99.9 8.7 %collective-permute-start = (bf16[4,2,1,384]{3,2,1,0:T(2,128)(2,1)S(1)}, bf16[4,2,1,384]{3,2,1,0:T(2,128)(2,1)S(1)}, u32[]{:S(2)}, u32[]{:S(2)}) collective-permute-start(bf16[4,2,1,384]{3,2,1,0:T(2,128)(2,1)S(1)} %get-tuple-element.518), channel_id=1, source_target_pairs={{0,1},{1,2},{2,3},{3,4},{4,5},{5,6},{6,7},{7,8},{8,9},{9,10},{10,1... | collective-permute-start | bytes 18440 | tf_op jit(solution)/shard_map/while/body/eval_jaxpr/ppermute | solution.py:14
  103.0 5.6 %collective-permute-start.1 = (bf16[4,2,1,384]{3,2,1,0:T(2,128)(2,1)S(1)}, bf16[4,2,1,384]{3,2,1,0:T(2,128)(2,1)S(1)}, u32[]{:S(2)}, u32[]{:S(2)}) collective-permute-start(bf16[4,2,1,384]{3,2,1,0:T(2,128)(2,1)S(1)} %get-tuple-element.519), channel_id=1, source_target_pairs={{1,0},{2,1},{3,2},{4,3},{5,4},{6,5},{7,6},{8,7},{9,8},{10,9},{11,1... | collective-permute-start | bytes 18440 | tf_op jit(solution)/shard_map/while/body/eval_jaxpr/ppermute | solution.py:17
  121.9 5.9 %collective-permute-start.2 = (bf16[2,4,2,8,384]{4,3,2,1,0:T(8,128)(2,1)S(1)}, bf16[2,4,2,8,384]{4,3,2,1,0:T(8,128)(2,1)S(1)}, u32[]{:S(2)}, u32[]{:S(2)}) collective-permute-start(bf16[2,4,2,8,384]{4,3,2,1,0:T(8,128)(2,1)S(1)} %pad_maximum_fusion.3), channel_id=1, source_target_pairs={{0,64},{64,128},{128,192},{192,256},{256,320},{320,384},{384,448},... | collective-permute-start | bytes 294920 | tf_op jit(solution)/shard_map/while/body/eval_jaxpr/ppermute | solution.py:25
  129.7 8.7 %collective-permute-start = (bf16[4,2,1,384]{3,2,1,0:T(2,128)(2,1)S(1)}, bf16[4,2,1,384]{3,2,1,0:T(2,128)(2,1)S(1)}, u32[]{:S(2)}, u32[]{:S(2)}) collective-permute-start(bf16[4,2,1,384]{3,2,1,0:T(2,128)(2,1)S(1)} %get-tuple-element.518), channel_id=1, source_target_pairs={{0,1},{1,2},{2,3},{3,4},{4,5},{5,6},{6,7},{7,8},{8,9},{9,10},{10,1... | collective-permute-start | bytes 18440 | tf_op jit(solution)/shard_map/while/body/eval_jaxpr/ppermute | solution.py:14
  132.8 5.6 %collective-permute-start.1 = (bf16[4,2,1,384]{3,2,1,0:T(2,128)(2,1)S(1)}, bf16[4,2,1,384]{3,2,1,0:T(2,128)(2,1)S(1)}, u32[]{:S(2)}, u32[]{:S(2)}) collective-permute-start(bf16[4,2,1,384]{3,2,1,0:T(2,128)(2,1)S(1)} %get-tuple-element.519), channel_id=1, source_target_pairs={{1,0},{2,1},{3,2},{4,3},{5,4},{6,5},{7,6},{8,7},{9,8},{10,9},{11,1... | collective-permute-start | bytes 18440 | tf_op jit(solution)/shard_map/while/body/eval_jaxpr/ppermute | solution.py:17
  151.8 5.9 %collective-permute-start.2 = (bf16[2,4,2,8,384]{4,3,2,1,0:T(8,128)(2,1)S(1)}, bf16[2,4,2,8,384]{4,3,2,1,0:T(8,128)(2,1)S(1)}, u32[]{:S(2)}, u32[]{:S(2)}) collective-permute-start(bf16[2,4,2,8,384]{4,3,2,1,0:T(8,128)(2,1)S(1)} %pad_maximum_fusion.3), channel_id=1, source_target_pairs={{0,64},{64,128},{128,192},{192,256},{256,320},{320,384},{384,448},... | collective-permute-start | bytes 294920 | tf_op jit(solution)/shard_map/while/body/eval_jaxpr/ppermute | solution.py:25
  159.5 8.9 %collective-permute-start = (bf16[4,2,1,384]{3,2,1,0:T(2,128)(2,1)S(1)}, bf16[4,2,1,384]{3,2,1,0:T(2,128)(2,1)S(1)}, u32[]{:S(2)}, u32[]{:S(2)}) collective-permute-start(bf16[4,2,1,384]{3,2,1,0:T(2,128)(2,1)S(1)} %get-tuple-element.518), channel_id=1, source_target_pairs={{0,1},{1,2},{2,3},{3,4},{4,5},{5,6},{6,7},{7,8},{8,9},{9,10},{10,1... | collective-permute-start | bytes 18440 | tf_op jit(solution)/shard_map/while/body/eval_jaxpr/ppermute | solution.py:14
  162.7 5.7 %collective-permute-start.1 = (bf16[4,2,1,384]{3,2,1,0:T(2,128)(2,1)S(1)}, bf16[4,2,1,384]{3,2,1,0:T(2,128)(2,1)S(1)}, u32[]{:S(2)}, u32[]{:S(2)}) collective-permute-start(bf16[4,2,1,384]{3,2,1,0:T(2,128)(2,1)S(1)} %get-tuple-element.519), channel_id=1, source_target_pairs={{1,0},{2,1},{3,2},{4,3},{5,4},{6,5},{7,6},{8,7},{9,8},{10,9},{11,1... | collective-permute-start | bytes 18440 | tf_op jit(solution)/shard_map/while/body/eval_jaxpr/ppermute | solution.py:17
  181.7 6.2 %collective-permute-start.2 = (bf16[2,4,2,8,384]{4,3,2,1,0:T(8,128)(2,1)S(1)}, bf16[2,4,2,8,384]{4,3,2,1,0:T(8,128)(2,1)S(1)}, u32[]{:S(2)}, u32[]{:S(2)}) collective-permute-start(bf16[2,4,2,8,384]{4,3,2,1,0:T(8,128)(2,1)S(1)} %pad_maximum_fusion.3), channel_id=1, source_target_pairs={{0,64},{64,128},{128,192},{192,256},{256,320},{320,384},{384,448},... | collective-permute-start | bytes 294920 | tf_op jit(solution)/shard_map/while/body/eval_jaxpr/ppermute | solution.py:25
  189.7 9.4 %collective-permute-start = (bf16[4,2,1,384]{3,2,1,0:T(2,128)(2,1)S(1)}, bf16[4,2,1,384]{3,2,1,0:T(2,128)(2,1)S(1)}, u32[]{:S(2)}, u32[]{:S(2)}) collective-permute-start(bf16[4,2,1,384]{3,2,1,0:T(2,128)(2,1)S(1)} %get-tuple-element.518), channel_id=1, source_target_pairs={{0,1},{1,2},{2,3},{3,4},{4,5},{5,6},{6,7},{7,8},{8,9},{9,10},{10,1... | collective-permute-start | bytes 18440 | tf_op jit(solution)/shard_map/while/body/eval_jaxpr/ppermute | solution.py:14
  193.4 5.7 %collective-permute-start.1 = (bf16[4,2,1,384]{3,2,1,0:T(2,128)(2,1)S(1)}, bf16[4,2,1,384]{3,2,1,0:T(2,128)(2,1)S(1)}, u32[]{:S(2)}, u32[]{:S(2)}) collective-permute-start(bf16[4,2,1,384]{3,2,1,0:T(2,128)(2,1)S(1)} %get-tuple-element.519), channel_id=1, source_target_pairs={{1,0},{2,1},{3,2},{4,3},{5,4},{6,5},{7,6},{8,7},{9,8},{10,9},{11,1... | collective-permute-start | bytes 18440 | tf_op jit(solution)/shard_map/while/body/eval_jaxpr/ppermute | solution.py:17
  212.4 6.2 %collective-permute-start.2 = (bf16[2,4,2,8,384]{4,3,2,1,0:T(8,128)(2,1)S(1)}, bf16[2,4,2,8,384]{4,3,2,1,0:T(8,128)(2,1)S(1)}, u32[]{:S(2)}, u32[]{:S(2)}) collective-permute-start(bf16[2,4,2,8,384]{4,3,2,1,0:T(8,128)(2,1)S(1)} %pad_maximum_fusion.3), channel_id=1, source_target_pairs={{0,64},{64,128},{128,192},{192,256},{256,320},{320,384},{384,448},... | collective-permute-start | bytes 294920 | tf_op jit(solution)/shard_map/while/body/eval_jaxpr/ppermute | solution.py:25
  220.4 9.7 %collective-permute-start = (bf16[4,2,1,384]{3,2,1,0:T(2,128)(2,1)S(1)}, bf16[4,2,1,384]{3,2,1,0:T(2,128)(2,1)S(1)}, u32[]{:S(2)}, u32[]{:S(2)}) collective-permute-start(bf16[4,2,1,384]{3,2,1,0:T(2,128)(2,1)S(1)} %get-tuple-element.518), channel_id=1, source_target_pairs={{0,1},{1,2},{2,3},{3,4},{4,5},{5,6},{6,7},{7,8},{8,9},{9,10},{10,1... | collective-permute-start | bytes 18440 | tf_op jit(solution)/shard_map/while/body/eval_jaxpr/ppermute | solution.py:14
  224.1 6.0 %collective-permute-start.1 = (bf16[4,2,1,384]{3,2,1,0:T(2,128)(2,1)S(1)}, bf16[4,2,1,384]{3,2,1,0:T(2,128)(2,1)S(1)}, u32[]{:S(2)}, u32[]{:S(2)}) collective-permute-start(bf16[4,2,1,384]{3,2,1,0:T(2,128)(2,1)S(1)} %get-tuple-element.519), channel_id=1, source_target_pairs={{1,0},{2,1},{3,2},{4,3},{5,4},{6,5},{7,6},{8,7},{9,8},{10,9},{11,1... | collective-permute-start | bytes 18440 | tf_op jit(solution)/shard_map/while/body/eval_jaxpr/ppermute | solution.py:17
  243.5 6.2 %collective-permute-start.2 = (bf16[2,4,2,8,384]{4,3,2,1,0:T(8,128)(2,1)S(1)}, bf16[2,4,2,8,384]{4,3,2,1,0:T(8,128)(2,1)S(1)}, u32[]{:S(2)}, u32[]{:S(2)}) collective-permute-start(bf16[2,4,2,8,384]{4,3,2,1,0:T(8,128)(2,1)S(1)} %pad_maximum_fusion.3), channel_id=1, source_target_pairs={{0,64},{64,128},{128,192},{192,256},{256,320},{320,384},{384,448},... | collective-permute-start | bytes 294920 | tf_op jit(solution)/shard_map/while/body/eval_jaxpr/ppermute | solution.py:25
  251.5 9.4 %collective-permute-start = (bf16[4,2,1,384]{3,2,1,0:T(2,128)(2,1)S(1)}, bf16[4,2,1,384]{3,2,1,0:T(2,128)(2,1)S(1)}, u32[]{:S(2)}, u32[]{:S(2)}) collective-permute-start(bf16[4,2,1,384]{3,2,1,0:T(2,128)(2,1)S(1)} %get-tuple-element.518), channel_id=1, source_target_pairs={{0,1},{1,2},{2,3},{3,4},{4,5},{5,6},{6,7},{7,8},{8,9},{9,10},{10,1... | collective-permute-start | bytes 18440 | tf_op jit(solution)/shard_map/while/body/eval_jaxpr/ppermute | solution.py:14
  255.1 5.7 %collective-permute-start.1 = (bf16[4,2,1,384]{3,2,1,0:T(2,128)(2,1)S(1)}, bf16[4,2,1,384]{3,2,1,0:T(2,128)(2,1)S(1)}, u32[]{:S(2)}, u32[]{:S(2)}) collective-permute-start(bf16[4,2,1,384]{3,2,1,0:T(2,128)(2,1)S(1)} %get-tuple-element.519), channel_id=1, source_target_pairs={{1,0},{2,1},{3,2},{4,3},{5,4},{6,5},{7,6},{8,7},{9,8},{10,9},{11,1... | collective-permute-start | bytes 18440 | tf_op jit(solution)/shard_map/while/body/eval_jaxpr/ppermute | solution.py:17
  274.2 6.2 %collective-permute-start.2 = (bf16[2,4,2,8,384]{4,3,2,1,0:T(8,128)(2,1)S(1)}, bf16[2,4,2,8,384]{4,3,2,1,0:T(8,128)(2,1)S(1)}, u32[]{:S(2)}, u32[]{:S(2)}) collective-permute-start(bf16[2,4,2,8,384]{4,3,2,1,0:T(8,128)(2,1)S(1)} %pad_maximum_fusion.3), channel_id=1, source_target_pairs={{0,64},{64,128},{128,192},{192,256},{256,320},{320,384},{384,448},... | collective-permute-start | bytes 294920 | tf_op jit(solution)/shard_map/while/body/eval_jaxpr/ppermute | solution.py:25
Sparse Core Ops, SparseCore 0:
  281.2 87.4 all-reduce.2
where the time goes:
time: 382 us; the launch traced here: 377 us
  waiting for transfers between devices  123 us (32%)
  matrix products  116 us (30%)
  starting transfers between devices  96.9 us (25%)
  other arithmetic  20.4 us (5%)
  between operations  15.3 us (4%)
    dot_general x81, matrix products, convolve(): jnp.dot(joined[frame_tap:frame_tap + frame_depth, row_tap:row_tap + row_c...  116 us
    psum x1, waiting for transfers between devices, from_root(): return lax.psum(jnp.where(mine, shard, jnp.zeros_like(shard)), axis)  87.6 us
    ppermute x9, starting transfers between devices, passed_along(): return lax.ppermute(block, axis, route)  41.1 us
    ppermute x9, starting transfers between devices, padded(): lax.ppermute(lax.slice_in_dim(block, block.shape[dim] - width, None, axis...  30.4 us
    ppermute x9, waiting for transfers between devices, padded(): lax.ppermute(lax.slice_in_dim(block, 0, width, axis=dim), axis, backward)  27.2 us
    ppermute x9, starting transfers between devices, padded(): lax.ppermute(lax.slice_in_dim(block, 0, width, axis=dim), axis, backward)  25.3 us
    reduce_sum x9, other arithmetic, advance(): jnp.mean(source * source, axis=-1, keepdims=True) + 1e-06  8.76 us
    ppermute x9, waiting for transfers between devices, passed_along(): return lax.ppermute(block, axis, route)  8.26 us
  transfers between devices with their start and end apart: 28, of which 19 were waited for; matrix products, arithmetic and copies ran while one was open for 0% of the time, Pallas kernels for 0%

commit v1 on v0

--- a/solution.py
+++ b/solution.py
@@ -27,7 +27,7 @@
 
 def from_root(shard, axis, root):
     mine = lax.axis_index(axis) == root
-    return lax.psum(jnp.where(mine, shard, jnp.zeros_like(shard)), axis)
+    return jnp.sum(lax.all_gather(jnp.where(mine, shard, jnp.zeros_like(shard)), axis), axis=0)
 
 
 def convolve(sequence, kernel, frame_depth, row_count, col_count):

time: 382 us -> 314 us (0.82)
  the two profiles are of different devices: /device:TPU:8 before, /device:TPU:249 now
where the time goes in v1:
time: 314 us; the launch traced here: 309 us
  matrix products  116 us (37%)
  starting transfers between devices  97.4 us (31%)
  waiting for transfers between devices  54.5 us (17%)
  other arithmetic  19.7 us (6%)
  blocking collectives  15 us (5%)
    dot_general x81, matrix products, convolve(): jnp.dot(joined[frame_tap:frame_tap + frame_depth, row_tap:row_tap + row_c...  116 us
    ppermute x9, starting transfers between devices, passed_along(): return lax.ppermute(block, axis, route)  48.8 us
    ppermute x9, waiting for transfers between devices, padded(): lax.ppermute(lax.slice_in_dim(block, 0, width, axis=dim), axis, backward)  39.9 us
    ppermute x9, starting transfers between devices, padded(): lax.ppermute(lax.slice_in_dim(block, 0, width, axis=dim), axis, backward)  28.8 us
    ppermute x9, starting transfers between devices, padded(): lax.ppermute(lax.slice_in_dim(block, block.shape[dim] - width, None, axis...  19.8 us
    all_gather x1, blocking collectives, from_root(): lax.all_gather(jnp.where(mine, shard, jnp.zeros_like(shard)), axis)  15 us
    ppermute x9, waiting for transfers between devices, passed_along(): return lax.ppermute(block, axis, route)  14.5 us
    reduce_sum x9, other arithmetic, advance(): jnp.mean(source * source, axis=-1, keepdims=True) + 1e-06  8.75 us
  transfers between devices with their start and end apart: 27, of which 18 were waited for; matrix products, arithmetic and copies ran while one was open for 0% of the time, Pallas kernels for 0%

profile of v1, /device:TPU:249, one launch (start us, length us, event | category | flops | bytes accessed | tf_op | source)
XLA Modules:
  0.0 308.8 jit_solution(3780561047105611739)
XLA Ops:
  3.9 289.2 %while.20 = (s32[]{:T(128)}, bf16[2,4,2,8,384]{4,3,2,1,0:T(8,128)(2,1)S(1)}, bf16[2,4,10,384]{3,2,1,0:T(8,128)(2,1)S(1)}, bf16[8,2,8,384]{3,2,1,0:T(8,128)(2,1)S...) while((s32[]{:T(128)}, ...), condition=%wide.region_2.3_spmd.clone, body=%wide.region_0.2_spmd.clone.sunk | while | flops 512637024 | bytes 16789532 | solution.py:110
  5.6 4.4 %collective-permute-start = (bf16[4,2,1,384]{3,2,1,0:T(2,128)(2,1)S(1)}, bf16[4,2,1,384]{3,2,1,0:T(2,128)(2,1)S(1)}, u32[]{:S(2)}, u32[]{:S(2)}) collective-permute-start(bf16[4,2,1,384]{3,2,1,0:T(2,128)(2,1)S(1)} %get-tuple-element.518), channel_id=1, source_target_pairs={{0,1},{1,2},{2,3},{3,4},{4,5},{5,6},{6,7},{7,8},{8,9},{9,10},{10,1... | collective-permute-start | bytes 18440 | tf_op jit(solution)/shard_map/while/body/eval_jaxpr/ppermute | solution.py:14
  10.1 1.9 collective-permute-start.1
  12.1 5.7 %collective-permute-done.1 = bf16[4,2,1,384]{3,2,1,0:T(2,128)(2,1)S(1)} collective-permute-done((bf16[4,2,1,384]{3,2,1,0:T(2,128)(2,1)S(1)}, bf16[4,2,1,384]{3,2,1,0:T(2,128)(2,1)S(1)}, u32[]{:S(2)}, u32[]{:S(2)}) %collective-permute-start.1) | collective-permute-done | bytes 6176 | tf_op jit(solution)/shard_map/while/body/eval_jaxpr/ppermute | solution.py:17
  31.2 5.1 %collective-permute-start.2 = (bf16[2,4,2,8,384]{4,3,2,1,0:T(8,128)(2,1)S(1)}, bf16[2,4,2,8,384]{4,3,2,1,0:T(8,128)(2,1)S(1)}, u32[]{:S(2)}, u32[]{:S(2)}) collective-permute-start(bf16[2,4,2,8,384]{4,3,2,1,0:T(8,128)(2,1)S(1)} %pad_maximum_fusion.3), channel_id=1, source_target_pairs={{0,64},{64,128},{128,192},{192,256},{256,320},{320,384},{384,448},... | collective-permute-start | bytes 294920 | tf_op jit(solution)/shard_map/while/body/eval_jaxpr/ppermute | solution.py:25
  36.3 1.6 collective-permute-done.2
  39.7 1.9 collective-permute-start
  41.6 3.4 %collective-permute-start.1 = (bf16[4,2,1,384]{3,2,1,0:T(2,128)(2,1)S(1)}, bf16[4,2,1,384]{3,2,1,0:T(2,128)(2,1)S(1)}, u32[]{:S(2)}, u32[]{:S(2)}) collective-permute-start(bf16[4,2,1,384]{3,2,1,0:T(2,128)(2,1)S(1)} %get-tuple-element.519), channel_id=1, source_target_pairs={{1,0},{2,1},{3,2},{4,3},{5,4},{6,5},{7,6},{8,7},{9,8},{10,9},{11,1... | collective-permute-start | bytes 18440 | tf_op jit(solution)/shard_map/while/body/eval_jaxpr/ppermute | solution.py:17
  45.1 4.3 %collective-permute-done.1 = bf16[4,2,1,384]{3,2,1,0:T(2,128)(2,1)S(1)} collective-permute-done((bf16[4,2,1,384]{3,2,1,0:T(2,128)(2,1)S(1)}, bf16[4,2,1,384]{3,2,1,0:T(2,128)(2,1)S(1)}, u32[]{:S(2)}, u32[]{:S(2)}) %collective-permute-start.1) | collective-permute-done | bytes 6176 | tf_op jit(solution)/shard_map/while/body/eval_jaxpr/ppermute | solution.py:17
  62.7 5.5 %collective-permute-start.2 = (bf16[2,4,2,8,384]{4,3,2,1,0:T(8,128)(2,1)S(1)}, bf16[2,4,2,8,384]{4,3,2,1,0:T(8,128)(2,1)S(1)}, u32[]{:S(2)}, u32[]{:S(2)}) collective-permute-start(bf16[2,4,2,8,384]{4,3,2,1,0:T(8,128)(2,1)S(1)} %pad_maximum_fusion.3), channel_id=1, source_target_pairs={{0,64},{64,128},{128,192},{192,256},{256,320},{320,384},{384,448},... | collective-permute-start | bytes 294920 | tf_op jit(solution)/shard_map/while/body/eval_jaxpr/ppermute | solution.py:25
  68.2 1.6 collective-permute-done.2
  71.6 1.9 collective-permute-start
  73.5 3.4 %collective-permute-start.1 = (bf16[4,2,1,384]{3,2,1,0:T(2,128)(2,1)S(1)}, bf16[4,2,1,384]{3,2,1,0:T(2,128)(2,1)S(1)}, u32[]{:S(2)}, u32[]{:S(2)}) collective-permute-start(bf16[4,2,1,384]{3,2,1,0:T(2,128)(2,1)S(1)} %get-tuple-element.519), channel_id=1, source_target_pairs={{1,0},{2,1},{3,2},{4,3},{5,4},{6,5},{7,6},{8,7},{9,8},{10,9},{11,1... | collective-permute-start | bytes 18440 | tf_op jit(solution)/shard_map/while/body/eval_jaxpr/ppermute | solution.py:17
  77.0 4.3 %collective-permute-done.1 = bf16[4,2,1,384]{3,2,1,0:T(2,128)(2,1)S(1)} collective-permute-done((bf16[4,2,1,384]{3,2,1,0:T(2,128)(2,1)S(1)}, bf16[4,2,1,384]{3,2,1,0:T(2,128)(2,1)S(1)}, u32[]{:S(2)}, u32[]{:S(2)}) %collective-permute-start.1) | collective-permute-done | bytes 6176 | tf_op jit(solution)/shard_map/while/body/eval_jaxpr/ppermute | solution.py:17
  94.6 5.5 %collective-permute-start.2 = (bf16[2,4,2,8,384]{4,3,2,1,0:T(8,128)(2,1)S(1)}, bf16[2,4,2,8,384]{4,3,2,1,0:T(8,128)(2,1)S(1)}, u32[]{:S(2)}, u32[]{:S(2)}) collective-permute-start(bf16[2,4,2,8,384]{4,3,2,1,0:T(8,128)(2,1)S(1)} %pad_maximum_fusion.3), channel_id=1, source_target_pairs={{0,64},{64,128},{128,192},{192,256},{256,320},{320,384},{384,448},... | collective-permute-start | bytes 294920 | tf_op jit(solution)/shard_map/while/body/eval_jaxpr/ppermute | solution.py:25
  100.1 1.6 collective-permute-done.2
  103.5 1.9 collective-permute-start
  105.4 3.4 %collective-permute-start.1 = (bf16[4,2,1,384]{3,2,1,0:T(2,128)(2,1)S(1)}, bf16[4,2,1,384]{3,2,1,0:T(2,128)(2,1)S(1)}, u32[]{:S(2)}, u32[]{:S(2)}) collective-permute-start(bf16[4,2,1,384]{3,2,1,0:T(2,128)(2,1)S(1)} %get-tuple-element.519), channel_id=1, source_target_pairs={{1,0},{2,1},{3,2},{4,3},{5,4},{6,5},{7,6},{8,7},{9,8},{10,9},{11,1... | collective-permute-start | bytes 18440 | tf_op jit(solution)/shard_map/while/body/eval_jaxpr/ppermute | solution.py:17
  108.9 4.3 %collective-permute-done.1 = bf16[4,2,1,384]{3,2,1,0:T(2,128)(2,1)S(1)} collective-permute-done((bf16[4,2,1,384]{3,2,1,0:T(2,128)(2,1)S(1)}, bf16[4,2,1,384]{3,2,1,0:T(2,128)(2,1)S(1)}, u32[]{:S(2)}, u32[]{:S(2)}) %collective-permute-start.1) | collective-permute-done | bytes 6176 | tf_op jit(solution)/shard_map/while/body/eval_jaxpr/ppermute | solution.py:17
  126.5 5.5 %collective-permute-start.2 = (bf16[2,4,2,8,384]{4,3,2,1,0:T(8,128)(2,1)S(1)}, bf16[2,4,2,8,384]{4,3,2,1,0:T(8,128)(2,1)S(1)}, u32[]{:S(2)}, u32[]{:S(2)}) collective-permute-start(bf16[2,4,2,8,384]{4,3,2,1,0:T(8,128)(2,1)S(1)} %pad_maximum_fusion.3), channel_id=1, source_target_pairs={{0,64},{64,128},{128,192},{192,256},{256,320},{320,384},{384,448},... | collective-permute-start | bytes 294920 | tf_op jit(solution)/shard_map/while/body/eval_jaxpr/ppermute | solution.py:25
  132.0 1.6 collective-permute-done.2
  135.4 1.9 collective-permute-start
  137.3 3.4 %collective-permute-start.1 = (bf16[4,2,1,384]{3,2,1,0:T(2,128)(2,1)S(1)}, bf16[4,2,1,384]{3,2,1,0:T(2,128)(2,1)S(1)}, u32[]{:S(2)}, u32[]{:S(2)}) collective-permute-start(bf16[4,2,1,384]{3,2,1,0:T(2,128)(2,1)S(1)} %get-tuple-element.519), channel_id=1, source_target_pairs={{1,0},{2,1},{3,2},{4,3},{5,4},{6,5},{7,6},{8,7},{9,8},{10,9},{11,1... | collective-permute-start | bytes 18440 | tf_op jit(solution)/shard_map/while/body/eval_jaxpr/ppermute | solution.py:17
  140.8 4.3 %collective-permute-done.1 = bf16[4,2,1,384]{3,2,1,0:T(2,128)(2,1)S(1)} collective-permute-done((bf16[4,2,1,384]{3,2,1,0:T(2,128)(2,1)S(1)}, bf16[4,2,1,384]{3,2,1,0:T(2,128)(2,1)S(1)}, u32[]{:S(2)}, u32[]{:S(2)}) %collective-permute-start.1) | collective-permute-done | bytes 6176 | tf_op jit(solution)/shard_map/while/body/eval_jaxpr/ppermute | solution.py:17
  156.9 1.5 select_dynamic-update-slice_fusion.2
  158.4 5.5 %collective-permute-start.2 = (bf16[2,4,2,8,384]{4,3,2,1,0:T(8,128)(2,1)S(1)}, bf16[2,4,2,8,384]{4,3,2,1,0:T(8,128)(2,1)S(1)}, u32[]{:S(2)}, u32[]{:S(2)}) collective-permute-start(bf16[2,4,2,8,384]{4,3,2,1,0:T(8,128)(2,1)S(1)} %pad_maximum_fusion.3), channel_id=1, source_target_pairs={{0,64},{64,128},{128,192},{192,256},{256,320},{320,384},{384,448},... | collective-permute-start | bytes 294920 | tf_op jit(solution)/shard_map/while/body/eval_jaxpr/ppermute | solution.py:25
  163.9 1.6 collective-permute-done.2
  167.3 1.9 collective-permute-start
  169.2 3.4 %collective-permute-start.1 = (bf16[4,2,1,384]{3,2,1,0:T(2,128)(2,1)S(1)}, bf16[4,2,1,384]{3,2,1,0:T(2,128)(2,1)S(1)}, u32[]{:S(2)}, u32[]{:S(2)}) collective-permute-start(bf16[4,2,1,384]{3,2,1,0:T(2,128)(2,1)S(1)} %get-tuple-element.519), channel_id=1, source_target_pairs={{1,0},{2,1},{3,2},{4,3},{5,4},{6,5},{7,6},{8,7},{9,8},{10,9},{11,1... | collective-permute-start | bytes 18440 | tf_op jit(solution)/shard_map/while/body/eval_jaxpr/ppermute | solution.py:17
  172.7 4.3 %collective-permute-done.1 = bf16[4,2,1,384]{3,2,1,0:T(2,128)(2,1)S(1)} collective-permute-done((bf16[4,2,1,384]{3,2,1,0:T(2,128)(2,1)S(1)}, bf16[4,2,1,384]{3,2,1,0:T(2,128)(2,1)S(1)}, u32[]{:S(2)}, u32[]{:S(2)}) %collective-permute-start.1) | collective-permute-done | bytes 6176 | tf_op jit(solution)/shard_map/while/body/eval_jaxpr/ppermute | solution.py:17
  190.3 5.5 %collective-permute-start.2 = (bf16[2,4,2,8,384]{4,3,2,1,0:T(8,128)(2,1)S(1)}, bf16[2,4,2,8,384]{4,3,2,1,0:T(8,128)(2,1)S(1)}, u32[]{:S(2)}, u32[]{:S(2)}) collective-permute-start(bf16[2,4,2,8,384]{4,3,2,1,0:T(8,128)(2,1)S(1)} %pad_maximum_fusion.3), channel_id=1, source_target_pairs={{0,64},{64,128},{128,192},{192,256},{256,320},{320,384},{384,448},... | collective-permute-start | bytes 294920 | tf_op jit(solution)/shard_map/while/body/eval_jaxpr/ppermute | solution.py:25
  195.8 1.6 collective-permute-done.2
  199.1 1.9 collective-permute-start
  201.1 3.4 %collective-permute-start.1 = (bf16[4,2,1,384]{3,2,1,0:T(2,128)(2,1)S(1)}, bf16[4,2,1,384]{3,2,1,0:T(2,128)(2,1)S(1)}, u32[]{:S(2)}, u32[]{:S(2)}) collective-permute-start(bf16[4,2,1,384]{3,2,1,0:T(2,128)(2,1)S(1)} %get-tuple-element.519), channel_id=1, source_target_pairs={{1,0},{2,1},{3,2},{4,3},{5,4},{6,5},{7,6},{8,7},{9,8},{10,9},{11,1... | collective-permute-start | bytes 18440 | tf_op jit(solution)/shard_map/while/body/eval_jaxpr/ppermute | solution.py:17
  204.6 4.3 %collective-permute-done.1 = bf16[4,2,1,384]{3,2,1,0:T(2,128)(2,1)S(1)} collective-permute-done((bf16[4,2,1,384]{3,2,1,0:T(2,128)(2,1)S(1)}, bf16[4,2,1,384]{3,2,1,0:T(2,128)(2,1)S(1)}, u32[]{:S(2)}, u32[]{:S(2)}) %collective-permute-start.1) | collective-permute-done | bytes 6176 | tf_op jit(solution)/shard_map/while/body/eval_jaxpr/ppermute | solution.py:17
  222.2 5.5 %collective-permute-start.2 = (bf16[2,4,2,8,384]{4,3,2,1,0:T(8,128)(2,1)S(1)}, bf16[2,4,2,8,384]{4,3,2,1,0:T(8,128)(2,1)S(1)}, u32[]{:S(2)}, u32[]{:S(2)}) collective-permute-start(bf16[2,4,2,8,384]{4,3,2,1,0:T(8,128)(2,1)S(1)} %pad_maximum_fusion.3), channel_id=1, source_target_pairs={{0,64},{64,128},{128,192},{192,256},{256,320},{320,384},{384,448},... | collective-permute-start | bytes 294920 | tf_op jit(solution)/shard_map/while/body/eval_jaxpr/ppermute | solution.py:25
  227.7 1.6 collective-permute-done.2
  231.0 1.9 collective-permute-start
  233.0 3.4 %collective-permute-start.1 = (bf16[4,2,1,384]{3,2,1,0:T(2,128)(2,1)S(1)}, bf16[4,2,1,384]{3,2,1,0:T(2,128)(2,1)S(1)}, u32[]{:S(2)}, u32[]{:S(2)}) collective-permute-start(bf16[4,2,1,384]{3,2,1,0:T(2,128)(2,1)S(1)} %get-tuple-element.519), channel_id=1, source_target_pairs={{1,0},{2,1},{3,2},{4,3},{5,4},{6,5},{7,6},{8,7},{9,8},{10,9},{11,1... | collective-permute-start | bytes 18440 | tf_op jit(solution)/shard_map/while/body/eval_jaxpr/ppermute | solution.py:17
  236.4 4.3 %collective-permute-done.1 = bf16[4,2,1,384]{3,2,1,0:T(2,128)(2,1)S(1)} collective-permute-done((bf16[4,2,1,384]{3,2,1,0:T(2,128)(2,1)S(1)}, bf16[4,2,1,384]{3,2,1,0:T(2,128)(2,1)S(1)}, u32[]{:S(2)}, u32[]{:S(2)}) %collective-permute-start.1) | collective-permute-done | bytes 6176 | tf_op jit(solution)/shard_map/while/body/eval_jaxpr/ppermute | solution.py:17
  254.1 5.5 %collective-permute-start.2 = (bf16[2,4,2,8,384]{4,3,2,1,0:T(8,128)(2,1)S(1)}, bf16[2,4,2,8,384]{4,3,2,1,0:T(8,128)(2,1)S(1)}, u32[]{:S(2)}, u32[]{:S(2)}) collective-permute-start(bf16[2,4,2,8,384]{4,3,2,1,0:T(8,128)(2,1)S(1)} %pad_maximum_fusion.3), channel_id=1, source_target_pairs={{0,64},{64,128},{128,192},{192,256},{256,320},{320,384},{384,448},... | collective-permute-start | bytes 294920 | tf_op jit(solution)/shard_map/while/body/eval_jaxpr/ppermute | solution.py:25
  259.5 1.6 collective-permute-done.2
  262.9 1.9 collective-permute-start
  264.9 3.4 %collective-permute-start.1 = (bf16[4,2,1,384]{3,2,1,0:T(2,128)(2,1)S(1)}, bf16[4,2,1,384]{3,2,1,0:T(2,128)(2,1)S(1)}, u32[]{:S(2)}, u32[]{:S(2)}) collective-permute-start(bf16[4,2,1,384]{3,2,1,0:T(2,128)(2,1)S(1)} %get-tuple-element.519), channel_id=1, source_target_pairs={{1,0},{2,1},{3,2},{4,3},{5,4},{6,5},{7,6},{8,7},{9,8},{10,9},{11,1... | collective-permute-start | bytes 18440 | tf_op jit(solution)/shard_map/while/body/eval_jaxpr/ppermute | solution.py:17
  268.3 4.3 %collective-permute-done.1 = bf16[4,2,1,384]{3,2,1,0:T(2,128)(2,1)S(1)} collective-permute-done((bf16[4,2,1,384]{3,2,1,0:T(2,128)(2,1)S(1)}, bf16[4,2,1,384]{3,2,1,0:T(2,128)(2,1)S(1)}, u32[]{:S(2)}, u32[]{:S(2)}) %collective-permute-start.1) | collective-permute-done | bytes 6176 | tf_op jit(solution)/shard_map/while/body/eval_jaxpr/ppermute | solution.py:17
  286.0 5.5 %collective-permute-start.2 = (bf16[2,4,2,8,384]{4,3,2,1,0:T(8,128)(2,1)S(1)}, bf16[2,4,2,8,384]{4,3,2,1,0:T(8,128)(2,1)S(1)}, u32[]{:S(2)}, u32[]{:S(2)}) collective-permute-start(bf16[2,4,2,8,384]{4,3,2,1,0:T(8,128)(2,1)S(1)} %pad_maximum_fusion.3), channel_id=1, source_target_pairs={{0,64},{64,128},{128,192},{192,256},{256,320},{320,384},{384,448},... | collective-permute-start | bytes 294920 | tf_op jit(solution)/shard_map/while/body/eval_jaxpr/ppermute | solution.py:25
  291.4 1.6 collective-permute-done.2
  293.1 15.0 %all-gather = bf16[64,2,8,384]{3,2,1,0:T(8,128)(2,1)S(1)} all-gather(bf16[8,2,8,384]{3,2,1,0:T(8,128)(2,1)S(1)} %broadcast_select_fusion.1), channel_id=2, replica_groups=mesh['section'=8,'tile'=64] {'section'}, dimensions={0}, use_global_device_ids=true | all-gather | bytes 884736 | tf_op jit(solution)/shard_map/all_gather | solution.py:30
  (223 shorter events, 136.8 us)
Async XLA Ops:
  5.6 12.2 %collective-permute-start = (bf16[4,2,1,384]{3,2,1,0:T(2,128)(2,1)S(1)}, bf16[4,2,1,384]{3,2,1,0:T(2,128)(2,1)S(1)}, u32[]{:S(2)}, u32[]{:S(2)}) collective-permute-start(bf16[4,2,1,384]{3,2,1,0:T(2,128)(2,1)S(1)} %get-tuple-element.518), channel_id=1, source_target_pairs={{0,1},{1,2},{2,3},{3,4},{4,5},{5,6},{6,7},{7,8},{8,9},{9,10},{10,1... | collective-permute-start | bytes 18440 | tf_op jit(solution)/shard_map/while/body/eval_jaxpr/ppermute | solution.py:14
  10.1 7.8 %collective-permute-start.1 = (bf16[4,2,1,384]{3,2,1,0:T(2,128)(2,1)S(1)}, bf16[4,2,1,384]{3,2,1,0:T(2,128)(2,1)S(1)}, u32[]{:S(2)}, u32[]{:S(2)}) collective-permute-start(bf16[4,2,1,384]{3,2,1,0:T(2,128)(2,1)S(1)} %get-tuple-element.519), channel_id=1, source_target_pairs={{1,0},{2,1},{3,2},{4,3},{5,4},{6,5},{7,6},{8,7},{9,8},{10,9},{11,1... | collective-permute-start | bytes 18440 | tf_op jit(solution)/shard_map/while/body/eval_jaxpr/ppermute | solution.py:17
  31.2 6.7 %collective-permute-start.2 = (bf16[2,4,2,8,384]{4,3,2,1,0:T(8,128)(2,1)S(1)}, bf16[2,4,2,8,384]{4,3,2,1,0:T(8,128)(2,1)S(1)}, u32[]{:S(2)}, u32[]{:S(2)}) collective-permute-start(bf16[2,4,2,8,384]{4,3,2,1,0:T(8,128)(2,1)S(1)} %pad_maximum_fusion.3), channel_id=1, source_target_pairs={{0,64},{64,128},{128,192},{192,256},{256,320},{320,384},{384,448},... | collective-permute-start | bytes 294920 | tf_op jit(solution)/shard_map/while/body/eval_jaxpr/ppermute | solution.py:25
  39.7 9.7 %collective-permute-start = (bf16[4,2,1,384]{3,2,1,0:T(2,128)(2,1)S(1)}, bf16[4,2,1,384]{3,2,1,0:T(2,128)(2,1)S(1)}, u32[]{:S(2)}, u32[]{:S(2)}) collective-permute-start(bf16[4,2,1,384]{3,2,1,0:T(2,128)(2,1)S(1)} %get-tuple-element.518), channel_id=1, source_target_pairs={{0,1},{1,2},{2,3},{3,4},{4,5},{5,6},{6,7},{7,8},{8,9},{9,10},{10,1... | collective-permute-start | bytes 18440 | tf_op jit(solution)/shard_map/while/body/eval_jaxpr/ppermute | solution.py:14
  41.6 7.8 %collective-permute-start.1 = (bf16[4,2,1,384]{3,2,1,0:T(2,128)(2,1)S(1)}, bf16[4,2,1,384]{3,2,1,0:T(2,128)(2,1)S(1)}, u32[]{:S(2)}, u32[]{:S(2)}) collective-permute-start(bf16[4,2,1,384]{3,2,1,0:T(2,128)(2,1)S(1)} %get-tuple-element.519), channel_id=1, source_target_pairs={{1,0},{2,1},{3,2},{4,3},{5,4},{6,5},{7,6},{8,7},{9,8},{10,9},{11,1... | collective-permute-start | bytes 18440 | tf_op jit(solution)/shard_map/while/body/eval_jaxpr/ppermute | solution.py:17
  62.7 7.1 %collective-permute-start.2 = (bf16[2,4,2,8,384]{4,3,2,1,0:T(8,128)(2,1)S(1)}, bf16[2,4,2,8,384]{4,3,2,1,0:T(8,128)(2,1)S(1)}, u32[]{:S(2)}, u32[]{:S(2)}) collective-permute-start(bf16[2,4,2,8,384]{4,3,2,1,0:T(8,128)(2,1)S(1)} %pad_maximum_fusion.3), channel_id=1, source_target_pairs={{0,64},{64,128},{128,192},{192,256},{256,320},{320,384},{384,448},... | collective-permute-start | bytes 294920 | tf_op jit(solution)/shard_map/while/body/eval_jaxpr/ppermute | solution.py:25
  71.6 9.7 %collective-permute-start = (bf16[4,2,1,384]{3,2,1,0:T(2,128)(2,1)S(1)}, bf16[4,2,1,384]{3,2,1,0:T(2,128)(2,1)S(1)}, u32[]{:S(2)}, u32[]{:S(2)}) collective-permute-start(bf16[4,2,1,384]{3,2,1,0:T(2,128)(2,1)S(1)} %get-tuple-element.518), channel_id=1, source_target_pairs={{0,1},{1,2},{2,3},{3,4},{4,5},{5,6},{6,7},{7,8},{8,9},{9,10},{10,1... | collective-permute-start | bytes 18440 | tf_op jit(solution)/shard_map/while/body/eval_jaxpr/ppermute | solution.py:14
  73.5 7.8 %collective-permute-start.1 = (bf16[4,2,1,384]{3,2,1,0:T(2,128)(2,1)S(1)}, bf16[4,2,1,384]{3,2,1,0:T(2,128)(2,1)S(1)}, u32[]{:S(2)}, u32[]{:S(2)}) collective-permute-start(bf16[4,2,1,384]{3,2,1,0:T(2,128)(2,1)S(1)} %get-tuple-element.519), channel_id=1, source_target_pairs={{1,0},{2,1},{3,2},{4,3},{5,4},{6,5},{7,6},{8,7},{9,8},{10,9},{11,1... | collective-permute-start | bytes 18440 | tf_op jit(solution)/shard_map/while/body/eval_jaxpr/ppermute | solution.py:17
  94.6 7.1 %collective-permute-start.2 = (bf16[2,4,2,8,384]{4,3,2,1,0:T(8,128)(2,1)S(1)}, bf16[2,4,2,8,384]{4,3,2,1,0:T(8,128)(2,1)S(1)}, u32[]{:S(2)}, u32[]{:S(2)}) collective-permute-start(bf16[2,4,2,8,384]{4,3,2,1,0:T(8,128)(2,1)S(1)} %pad_maximum_fusion.3), channel_id=1, source_target_pairs={{0,64},{64,128},{128,192},{192,256},{256,320},{320,384},{384,448},... | collective-permute-start | bytes 294920 | tf_op jit(solution)/shard_map/while/body/eval_jaxpr/ppermute | solution.py:25
  103.5 9.7 %collective-permute-start = (bf16[4,2,1,384]{3,2,1,0:T(2,128)(2,1)S(1)}, bf16[4,2,1,384]{3,2,1,0:T(2,128)(2,1)S(1)}, u32[]{:S(2)}, u32[]{:S(2)}) collective-permute-start(bf16[4,2,1,384]{3,2,1,0:T(2,128)(2,1)S(1)} %get-tuple-element.518), channel_id=1, source_target_pairs={{0,1},{1,2},{2,3},{3,4},{4,5},{5,6},{6,7},{7,8},{8,9},{9,10},{10,1... | collective-permute-start | bytes 18440 | tf_op jit(solution)/shard_map/while/body/eval_jaxpr/ppermute | solution.py:14
  105.4 7.8 %collective-permute-start.1 = (bf16[4,2,1,384]{3,2,1,0:T(2,128)(2,1)S(1)}, bf16[4,2,1,384]{3,2,1,0:T(2,128)(2,1)S(1)}, u32[]{:S(2)}, u32[]{:S(2)}) collective-permute-start(bf16[4,2,1,384]{3,2,1,0:T(2,128)(2,1)S(1)} %get-tuple-element.519), channel_id=1, source_target_pairs={{1,0},{2,1},{3,2},{4,3},{5,4},{6,5},{7,6},{8,7},{9,8},{10,9},{11,1... | collective-permute-start | bytes 18440 | tf_op jit(solution)/shard_map/while/body/eval_jaxpr/ppermute | solution.py:17
  126.5 7.1 %collective-permute-start.2 = (bf16[2,4,2,8,384]{4,3,2,1,0:T(8,128)(2,1)S(1)}, bf16[2,4,2,8,384]{4,3,2,1,0:T(8,128)(2,1)S(1)}, u32[]{:S(2)}, u32[]{:S(2)}) collective-permute-start(bf16[2,4,2,8,384]{4,3,2,1,0:T(8,128)(2,1)S(1)} %pad_maximum_fusion.3), channel_id=1, source_target_pairs={{0,64},{64,128},{128,192},{192,256},{256,320},{320,384},{384,448},... | collective-permute-start | bytes 294920 | tf_op jit(solution)/shard_map/while/body/eval_jaxpr/ppermute | solution.py:25
  135.4 9.7 %collective-permute-start = (bf16[4,2,1,384]{3,2,1,0:T(2,128)(2,1)S(1)}, bf16[4,2,1,384]{3,2,1,0:T(2,128)(2,1)S(1)}, u32[]{:S(2)}, u32[]{:S(2)}) collective-permute-start(bf16[4,2,1,384]{3,2,1,0:T(2,128)(2,1)S(1)} %get-tuple-element.518), channel_id=1, source_target_pairs={{0,1},{1,2},{2,3},{3,4},{4,5},{5,6},{6,7},{7,8},{8,9},{9,10},{10,1... | collective-permute-start | bytes 18440 | tf_op jit(solution)/shard_map/while/body/eval_jaxpr/ppermute | solution.py:14
  137.3 7.8 %collective-permute-start.1 = (bf16[4,2,1,384]{3,2,1,0:T(2,128)(2,1)S(1)}, bf16[4,2,1,384]{3,2,1,0:T(2,128)(2,1)S(1)}, u32[]{:S(2)}, u32[]{:S(2)}) collective-permute-start(bf16[4,2,1,384]{3,2,1,0:T(2,128)(2,1)S(1)} %get-tuple-element.519), channel_id=1, source_target_pairs={{1,0},{2,1},{3,2},{4,3},{5,4},{6,5},{7,6},{8,7},{9,8},{10,9},{11,1... | collective-permute-start | bytes 18440 | tf_op jit(solution)/shard_map/while/body/eval_jaxpr/ppermute | solution.py:17
  158.4 7.1 %collective-permute-start.2 = (bf16[2,4,2,8,384]{4,3,2,1,0:T(8,128)(2,1)S(1)}, bf16[2,4,2,8,384]{4,3,2,1,0:T(8,128)(2,1)S(1)}, u32[]{:S(2)}, u32[]{:S(2)}) collective-permute-start(bf16[2,4,2,8,384]{4,3,2,1,0:T(8,128)(2,1)S(1)} %pad_maximum_fusion.3), channel_id=1, source_target_pairs={{0,64},{64,128},{128,192},{192,256},{256,320},{320,384},{384,448},... | collective-permute-start | bytes 294920 | tf_op jit(solution)/shard_map/while/body/eval_jaxpr/ppermute | solution.py:25
  167.3 9.7 %collective-permute-start = (bf16[4,2,1,384]{3,2,1,0:T(2,128)(2,1)S(1)}, bf16[4,2,1,384]{3,2,1,0:T(2,128)(2,1)S(1)}, u32[]{:S(2)}, u32[]{:S(2)}) collective-permute-start(bf16[4,2,1,384]{3,2,1,0:T(2,128)(2,1)S(1)} %get-tuple-element.518), channel_id=1, source_target_pairs={{0,1},{1,2},{2,3},{3,4},{4,5},{5,6},{6,7},{7,8},{8,9},{9,10},{10,1... | collective-permute-start | bytes 18440 | tf_op jit(solution)/shard_map/while/body/eval_jaxpr/ppermute | solution.py:14
  169.2 7.8 %collective-permute-start.1 = (bf16[4,2,1,384]{3,2,1,0:T(2,128)(2,1)S(1)}, bf16[4,2,1,384]{3,2,1,0:T(2,128)(2,1)S(1)}, u32[]{:S(2)}, u32[]{:S(2)}) collective-permute-start(bf16[4,2,1,384]{3,2,1,0:T(2,128)(2,1)S(1)} %get-tuple-element.519), channel_id=1, source_target_pairs={{1,0},{2,1},{3,2},{4,3},{5,4},{6,5},{7,6},{8,7},{9,8},{10,9},{11,1... | collective-permute-start | bytes 18440 | tf_op jit(solution)/shard_map/while/body/eval_jaxpr/ppermute | solution.py:17
  190.3 7.1 %collective-permute-start.2 = (bf16[2,4,2,8,384]{4,3,2,1,0:T(8,128)(2,1)S(1)}, bf16[2,4,2,8,384]{4,3,2,1,0:T(8,128)(2,1)S(1)}, u32[]{:S(2)}, u32[]{:S(2)}) collective-permute-start(bf16[2,4,2,8,384]{4,3,2,1,0:T(8,128)(2,1)S(1)} %pad_maximum_fusion.3), channel_id=1, source_target_pairs={{0,64},{64,128},{128,192},{192,256},{256,320},{320,384},{384,448},... | collective-permute-start | bytes 294920 | tf_op jit(solution)/shard_map/while/body/eval_jaxpr/ppermute | solution.py:25
  199.1 9.7 %collective-permute-start = (bf16[4,2,1,384]{3,2,1,0:T(2,128)(2,1)S(1)}, bf16[4,2,1,384]{3,2,1,0:T(2,128)(2,1)S(1)}, u32[]{:S(2)}, u32[]{:S(2)}) collective-permute-start(bf16[4,2,1,384]{3,2,1,0:T(2,128)(2,1)S(1)} %get-tuple-element.518), channel_id=1, source_target_pairs={{0,1},{1,2},{2,3},{3,4},{4,5},{5,6},{6,7},{7,8},{8,9},{9,10},{10,1... | collective-permute-start | bytes 18440 | tf_op jit(solution)/shard_map/while/body/eval_jaxpr/ppermute | solution.py:14
  201.1 7.8 %collective-permute-start.1 = (bf16[4,2,1,384]{3,2,1,0:T(2,128)(2,1)S(1)}, bf16[4,2,1,384]{3,2,1,0:T(2,128)(2,1)S(1)}, u32[]{:S(2)}, u32[]{:S(2)}) collective-permute-start(bf16[4,2,1,384]{3,2,1,0:T(2,128)(2,1)S(1)} %get-tuple-element.519), channel_id=1, source_target_pairs={{1,0},{2,1},{3,2},{4,3},{5,4},{6,5},{7,6},{8,7},{9,8},{10,9},{11,1... | collective-permute-start | bytes 18440 | tf_op jit(solution)/shard_map/while/body/eval_jaxpr/ppermute | solution.py:17
  222.2 7.1 %collective-permute-start.2 = (bf16[2,4,2,8,384]{4,3,2,1,0:T(8,128)(2,1)S(1)}, bf16[2,4,2,8,384]{4,3,2,1,0:T(8,128)(2,1)S(1)}, u32[]{:S(2)}, u32[]{:S(2)}) collective-permute-start(bf16[2,4,2,8,384]{4,3,2,1,0:T(8,128)(2,1)S(1)} %pad_maximum_fusion.3), channel_id=1, source_target_pairs={{0,64},{64,128},{128,192},{192,256},{256,320},{320,384},{384,448},... | collective-permute-start | bytes 294920 | tf_op jit(solution)/shard_map/while/body/eval_jaxpr/ppermute | solution.py:25
  231.0 9.7 %collective-permute-start = (bf16[4,2,1,384]{3,2,1,0:T(2,128)(2,1)S(1)}, bf16[4,2,1,384]{3,2,1,0:T(2,128)(2,1)S(1)}, u32[]{:S(2)}, u32[]{:S(2)}) collective-permute-start(bf16[4,2,1,384]{3,2,1,0:T(2,128)(2,1)S(1)} %get-tuple-element.518), channel_id=1, source_target_pairs={{0,1},{1,2},{2,3},{3,4},{4,5},{5,6},{6,7},{7,8},{8,9},{9,10},{10,1... | collective-permute-start | bytes 18440 | tf_op jit(solution)/shard_map/while/body/eval_jaxpr/ppermute | solution.py:14
  233.0 7.8 %collective-permute-start.1 = (bf16[4,2,1,384]{3,2,1,0:T(2,128)(2,1)S(1)}, bf16[4,2,1,384]{3,2,1,0:T(2,128)(2,1)S(1)}, u32[]{:S(2)}, u32[]{:S(2)}) collective-permute-start(bf16[4,2,1,384]{3,2,1,0:T(2,128)(2,1)S(1)} %get-tuple-element.519), channel_id=1, source_target_pairs={{1,0},{2,1},{3,2},{4,3},{5,4},{6,5},{7,6},{8,7},{9,8},{10,9},{11,1... | collective-permute-start | bytes 18440 | tf_op jit(solution)/shard_map/while/body/eval_jaxpr/ppermute | solution.py:17
  254.1 7.1 %collective-permute-start.2 = (bf16[2,4,2,8,384]{4,3,2,1,0:T(8,128)(2,1)S(1)}, bf16[2,4,2,8,384]{4,3,2,1,0:T(8,128)(2,1)S(1)}, u32[]{:S(2)}, u32[]{:S(2)}) collective-permute-start(bf16[2,4,2,8,384]{4,3,2,1,0:T(8,128)(2,1)S(1)} %pad_maximum_fusion.3), channel_id=1, source_target_pairs={{0,64},{64,128},{128,192},{192,256},{256,320},{320,384},{384,448},... | collective-permute-start | bytes 294920 | tf_op jit(solution)/shard_map/while/body/eval_jaxpr/ppermute | solution.py:25
  262.9 9.7 %collective-permute-start = (bf16[4,2,1,384]{3,2,1,0:T(2,128)(2,1)S(1)}, bf16[4,2,1,384]{3,2,1,0:T(2,128)(2,1)S(1)}, u32[]{:S(2)}, u32[]{:S(2)}) collective-permute-start(bf16[4,2,1,384]{3,2,1,0:T(2,128)(2,1)S(1)} %get-tuple-element.518), channel_id=1, source_target_pairs={{0,1},{1,2},{2,3},{3,4},{4,5},{5,6},{6,7},{7,8},{8,9},{9,10},{10,1... | collective-permute-start | bytes 18440 | tf_op jit(solution)/shard_map/while/body/eval_jaxpr/ppermute | solution.py:14
  264.9 7.8 %collective-permute-start.1 = (bf16[4,2,1,384]{3,2,1,0:T(2,128)(2,1)S(1)}, bf16[4,2,1,384]{3,2,1,0:T(2,128)(2,1)S(1)}, u32[]{:S(2)}, u32[]{:S(2)}) collective-permute-start(bf16[4,2,1,384]{3,2,1,0:T(2,128)(2,1)S(1)} %get-tuple-element.519), channel_id=1, source_target_pairs={{1,0},{2,1},{3,2},{4,3},{5,4},{6,5},{7,6},{8,7},{9,8},{10,9},{11,1... | collective-permute-start | bytes 18440 | tf_op jit(solution)/shard_map/while/body/eval_jaxpr/ppermute | solution.py:17
  286.0 7.1 %collective-permute-start.2 = (bf16[2,4,2,8,384]{4,3,2,1,0:T(8,128)(2,1)S(1)}, bf16[2,4,2,8,384]{4,3,2,1,0:T(8,128)(2,1)S(1)}, u32[]{:S(2)}, u32[]{:S(2)}) collective-permute-start(bf16[2,4,2,8,384]{4,3,2,1,0:T(8,128)(2,1)S(1)} %pad_maximum_fusion.3), channel_id=1, source_target_pairs={{0,64},{64,128},{128,192},{192,256},{256,320},{320,384},{384,448},... | collective-permute-start | bytes 294920 | tf_op jit(solution)/shard_map/while/body/eval_jaxpr/ppermute | solution.py:25
